TPU v7x, 32 devices: a whole 2x2x4 slice. The times are simulated.
32 devices in a mesh: well: 4 (over y, x), tile: 8 (over z, core).
Axes of the slice: x: 2, y: 2, z: 4, core: 2. Of those that a mesh axis runs over, the one named last changes fastest.
Arguments:
- prior_state: float32 [3, 200, 8192], P(None, None, 'tile'), may hold values from -6 to 6
- pred_data: float32 [4096, 200], P(('well', 'tile')), may hold values from -6 to 6
- obs_pert: float32 [4096, 200], P(('well', 'tile')), may hold values from -12 to 12
- obs_std: float32 [4096], P(('well', 'tile')), may hold values from 0.5 to 2
- loc_mask: int32 [8, 32], P('tile', 'well'), may hold values from 0 to 1, as said below
- taper_level: int32 [8, 32], P('tile', 'well'), may hold values from 1 to 4
Outputs:
- analysis: float32 [3, 200, 8192], P(None, 'well', 'tile')
Inputs may be any that keep to these rules, and one draw needn't show every extreme that they name: `loc_mask`: each tile is localized to a set of data blocks whose size varies strongly from tile to tile; some tile is localized to most blocks.
All inputs are finite; a program needn't handle non-finite values.
Results may differ from a plain program's by a relative error of at most 0.0003.
Values sent between devices are 32-bit elements; how exact they have to be, the bound alone decides.
No kernel may reach another device: no remote copies, remote signals or barrier semaphores. Data moves between devices by JAX's collectives and lax.ppermute only.
A program may use at most 64 MiB of HBM per device.

v0:
```python
import jax
import jax.numpy as jnp
from jax import lax
from jax.sharding import PartitionSpec as P

BLOCK = 128


def chol_apply(system, right):
    factor = jnp.linalg.cholesky(system)
    middle = lax.linalg.triangular_solve(
        factor, right, left_side=True, lower=True, transpose_a=False
    )
    return lax.linalg.triangular_solve(factor, middle, left_side=True, lower=True, transpose_a=True)


def prepare(pred_rows, obs_rows, std_rows, norm_factor):
    data_anom = (pred_rows - jnp.mean(pred_rows, axis=1, keepdims=True)) * norm_factor
    innov = obs_rows - pred_rows
    row_weight = 1.0 / (4.0 * std_rows * std_rows)
    scaled = row_weight[:, None] * data_anom
    return (data_anom, innov, row_weight, scaled)


def shards(prior_state, pred_data, obs_pert, obs_std, loc_mask, taper_level):
    highest = lax.Precision.HIGHEST
    members = pred_data.shape[1]
    norm_factor = 1.0 / jnp.sqrt(jnp.float32(members - 1))
    data_anom, innov, row_weight, scaled = prepare(pred_data, obs_pert, obs_std, norm_factor)
    gram_matrix, cross_matrix = lax.psum(
        (
            jnp.dot(data_anom.T, scaled, precision=highest),
            jnp.dot(scaled.T, innov, precision=highest),
        ),
        ("well", "tile"),
    )
    system = jnp.eye(members, dtype=jnp.float32) + gram_matrix
    solved = chol_apply(system, cross_matrix)
    gain_rows = row_weight[:, None] * innov - jnp.dot(scaled, solved, precision=highest)
    group_anom, group_gain = (
        lax.all_gather(data_anom, "tile", axis=0, tiled=True),
        lax.all_gather(gain_rows, "tile", axis=0, tiled=True),
    )
    taper_row = loc_mask[0].astype(jnp.float32) * taper_level[0].astype(jnp.float32) / 4.0
    state_anom = (prior_state - jnp.mean(prior_state, axis=1, keepdims=True)) * norm_factor
    own_count = members // lax.axis_size("well")
    own_start = lax.axis_index("well") * own_count
    row_taper = jnp.repeat(taper_row, BLOCK)
    space = jnp.dot((group_anom * row_taper[:, None]).T, group_gain, precision=highest)
    space_mine = lax.psum_scatter(space, "well", scatter_dimension=1, tiled=True)
    increment = jnp.einsum("vnc,nm->vmc", state_anom, space_mine, precision=highest)
    prior_mine = lax.dynamic_slice_in_dim(prior_state, own_start, own_count, 1)
    return prior_mine + increment


def solution(mesh):
    return jax.shard_map(
        shards,
        mesh=mesh,
        in_specs=(
            P(None, None, "tile"),
            P(("well", "tile"), None),
            P(("well", "tile"), None),
            P(("well", "tile")),
            P("tile", "well"),
            P("tile", "well"),
        ),
        out_specs=P(None, "well", "tile"),
        check_vma=False,
    )
```

profile of v0, /device:TPU:4, one launch (start us, length us, event | category | flops | bytes accessed | tf_op | source)
XLA Modules:
  0.0 278.2 jit_solution(14750965140446197229)
XLA Ops:
  6.5 1.1 reduce_sum.18
  7.6 1.2 broadcast_multiply_fusion.1
  8.8 2.0 fusion.22
  10.8 2.0 fusion.21
  12.8 0.0 all-reduce.8.cloned.1.call-update
  12.9 0.9 subtract_multiply_fusion.1
  13.8 16.0 %all_gather.6 = f32[1024,200]{0,1:T(8,128)S(1)} all-gather(f32[128,200]{0,1:T(8,128)S(1)} %subtract_multiply_fusion.1), channel_id=1, replica_groups=mesh['well'=4,'tile'=8] {'tile'}, dimensions={0}, use_global_device_ids=true | all-gather | bytes 921600 | tf_op jit(solution)/shard_map/all_gather | solution.py:41
  29.8 0.1 broadcast_bitcast_fusion
  29.9 0.8 reduce_sum.19
  30.6 110.1 %all-reduce.8.cloned.1.call-done = (f32[200,200]{1,0:T(8,128)}, f32[200,200]{0,1:T(8,128)}) async-done(((f32[200,200]{1,0:T(8,128)}, f32[200,200]{0,1:T(8,128)}), (f32[200,200]{1,0:T(8,128)}, f32[200,200]{0,1:T(8,128)})) %all-reduce.8.cloned.1.call-update) | async-done | bytes 320016 | tf_op jit(solution)/shard_map/psum | solution.py:30
  140.7 1.7 convert_add_fusion
  142.4 1.7 copy.10
  144.1 1.1 fusion.18
  145.2 0.0 copy-start.3
  145.2 0.7 copy-done.3
  145.9 0.6 cholesky.124
  146.5 13.2 %cholesky.51 = f32[128,128]{1,0:T(8,128)} custom-call(f32[128,128]{1,0:T(8,128)} %cholesky.124), custom_call_target="Cholesky" | custom-call | tf_op jit(solution)/shard_map/jit(cholesky)/cholesky | solution.py:10
  159.7 2.0 select_reduce_fusion
  161.7 1.5 cholesky.119
  163.2 11.3 %custom-call.16 = f32[1,128,128]{1,2,0:T(8,128)} custom-call(f32[1,128,128]{2,1,0:T(8,128)} %get-tuple-element.30), custom_call_target="InvertDiagBlocksLowerTriangular" | custom-call | tf_op jit(solution)/shard_map/jit(cholesky)/cholesky | solution.py:10
  174.5 1.7 constant_dynamic-update-slice_fusion.1
  176.2 1.6 convolution_subtract_fusion.3
  177.8 8.0 %cholesky.110 = f32[72,72]{1,0:T(8,128)} custom-call(f32[72,72]{1,0:T(8,128)} %convolution_subtract_fusion.3), custom_call_target="Cholesky" | custom-call | tf_op jit(solution)/shard_map/jit(cholesky)/cholesky | solution.py:10
  185.7 1.4 select_reduce_fusion.1
  187.1 0.6 compare_reduce_fusion
  187.8 1.3 compare_reduce_fusion.1
  190.3 1.0 select_select_fusion
  191.2 0.0 copy-start.2
  191.3 0.7 copy-done.2
  191.9 0.1 fusion.23
  192.0 0.7 pad_maximum_fusion
  192.7 21.1 %custom-call.17 = f32[2,128,128]{1,2,0:T(8,128)} custom-call(f32[2,128,128]{2,1,0:T(8,128)} %pad_maximum_fusion), custom_call_target="InvertDiagBlocksLowerTriangular" | custom-call | tf_op jit(solution)/shard_map/triangular_solve | solution.py:14
  213.8 1.4 fusion.19
  215.1 0.0 copy-start.7
  215.2 1.2 convolution_subtract_fusion.2
  216.4 1.0 fusion.36
  217.4 1.0 fusion.35
  218.4 1.1 convolution_subtract_fusion
  219.6 1.2 fusion.26
  220.8 1.2 convolution_subtract_fusion.1
  222.0 17.3 %all_gather.7 = f32[1024,200]{0,1:T(8,128)S(1)} all-gather(f32[128,200]{0,1:T(8,128)S(1)} %convolution_subtract_fusion.1), channel_id=1, replica_groups=mesh['well'=4,'tile'=8] {'tile'}, dimensions={0}, use_global_device_ids=true | all-gather | bytes 921600 | tf_op jit(solution)/shard_map/all_gather | solution.py:42
  239.3 0.9 fusion.12
  240.2 21.4 %fusion = f32[200,64]{0,1:T(8,128)S(1)} fusion(f32[200,200]{0,1:T(8,128)S(1)} %fusion.12), kind=kCustom, calls=%all-reduce-scatter | all-reduce-scatter fusion | flops 51201 | bytes 211712
  261.7 3.4 %collective-permute-start = (f32[200,42]{0,1:T(8,128)S(1)}, f32[200,42]{0,1:T(8,128)S(1)}, u32[]{:S(2)}, u32[]{:S(2)}) collective-permute-start(f32[200,42]{0,1:T(8,128)S(1)} %slice.74), channel_id=1, source_target_pairs={{0,8},{8,16},{16,24},{1,9},{9,17},{17,25},{2,10},{10,18},{18,26},{... | collective-permute-start | bytes 100808
  265.1 0.6 dynamic-slice.8
  266.3 2.2 collective-permute-done
  268.5 0.2 concatenate.13
  268.7 2.6 fusion.7
  (23 shorter events, 0.1 us)
Async XLA Ops:
  6.5 23.3 %copy-start.9 = (s32[1,8]{1,0:T(1,128)S(1)}, s32[1,8]{1,0:T(1,128)}, u32[]{:S(2)}) copy-start(s32[1,8]{1,0:T(1,128)} %param.10) | copy-start | bytes 100
  6.5 23.3 %copy-start.8 = (s32[1,8]{1,0:T(1,128)S(1)}, s32[1,8]{1,0:T(1,128)}, u32[]{:S(2)}) copy-start(s32[1,8]{1,0:T(1,128)} %param.11) | copy-start | bytes 100
  6.5 23.3 %copy-start = (f32[3,200,1024]{2,1,0:T(8,128)S(1)}, f32[3,200,1024]{2,1,0:T(8,128)}, u32[]{:S(2)}) copy-start(f32[3,200,1024]{2,1,0:T(8,128)} %param.6) | copy-start | bytes 7372804
  6.5 134.2 %all-reduce.8.cloned.1.call-start = ((), (), s32[]{:S(2)}) async-start(), calls=%async_computation | async-start | bytes 819200 | tf_op jit(solution)/shard_map/psum | solution.py:30
  8.8 2.0 copy-start.6
  140.7 80.0 %copy-start.1 = (f32[128,200]{0,1:T(8,128)S(1)}, f32[128,200]{0,1:T(8,128)}, u32[]{:S(2)}) copy-start(f32[128,200]{0,1:T(8,128)} %param.7) | copy-start | bytes 307204
  140.7 80.0 %copy-start.4 = (f32[128,200]{0,1:T(8,128)S(1)}, f32[128,200]{0,1:T(8,128)}, u32[]{:S(2)}) copy-start(f32[128,200]{0,1:T(8,128)} %param.8) | copy-start | bytes 307204
  145.2 0.7 copy-start.3
  191.2 0.7 copy-start.2
  215.1 49.9 %copy-start.5 = (f32[3,1024]{1,0:T(4,128)S(1)}, f32[3,1024]{1,0:T(4,128)}, u32[]{:S(2)}) copy-start(f32[3,1024]{1,0:T(4,128)} %reduce_sum.19) | copy-start | bytes 36868
  215.1 49.9 %copy-start.7 = (u32[32]{0:T(128)S(1)}, u32[32]{0:T(128)}, u32[]{:S(2)}) copy-start(u32[32]{0:T(128)} %constant.155) | copy-start | bytes 388
  261.7 6.9 %collective-permute-start = (f32[200,42]{0,1:T(8,128)S(1)}, f32[200,42]{0,1:T(8,128)S(1)}, u32[]{:S(2)}, u32[]{:S(2)}) collective-permute-start(f32[200,42]{0,1:T(8,128)S(1)} %slice.74), channel_id=1, source_target_pairs={{0,8},{8,16},{16,24},{1,9},{9,17},{17,25},{2,10},{10,18},{18,26},{... | collective-permute-start | bytes 100808
Sparse Core Ops, SparseCore 0:
  13.0 127.6 all-reduce.7
where the time goes:
time: 279 us; the launch traced here: 278 us
  waiting for transfers between devices  112 us (40%)
  other arithmetic  67.3 us (24%)
  blocking collectives  54.7 us (20%)
  matrix products  19 us (7%)
  between operations  15.4 us (6%)
  local copies, waits for them, and re-layouts  6.12 us (2%)
  starting transfers between devices  3.37 us (1%)
    psum x1, waiting for transfers between devices, shards(): lax.psum((jnp.dot(data_anom.T, scaled, precision=highest), jnp.dot(scaled...  110 us
    another operation x7, other arithmetic, chol_apply(): factor = jnp.linalg.cholesky(system)  37.8 us
    another operation x6, other arithmetic, chol_apply(): lax.linalg.triangular_solve(factor, middle, left_side=True, lower=True, t...  22.8 us
    unnamed x1, blocking collectives  21.4 us
    all_gather x1, blocking collectives, shards(): lax.all_gather(gain_rows, 'tile', axis=0, tiled=True)  17.3 us
    all_gather x1, blocking collectives, shards(): lax.all_gather(data_anom, 'tile', axis=0, tiled=True)  16 us
  transfers between devices with their start and end apart: 2, of which 2 were waited for; matrix products, arithmetic and copies ran while one was open for 1% of the time, Pallas kernels for 0%

commit v1 on v0

--- a/solution.py
+++ b/solution.py
@@ -28,11 +28,14 @@
     norm_factor = 1.0 / jnp.sqrt(jnp.float32(members - 1))
     data_anom, innov, row_weight, scaled = prepare(pred_data, obs_pert, obs_std, norm_factor)
     gram_matrix, cross_matrix = lax.psum(
-        (
-            jnp.dot(data_anom.T, scaled, precision=highest),
-            jnp.dot(scaled.T, innov, precision=highest),
+        lax.psum(
+            (
+                jnp.dot(data_anom.T, scaled, precision=highest),
+                jnp.dot(scaled.T, innov, precision=highest),
+            ),
+            "tile",
         ),
-        ("well", "tile"),
+        "well",
     )
     system = jnp.eye(members, dtype=jnp.float32) + gram_matrix
     solved = chol_apply(system, cross_matrix)

time: 279 us -> 233 us (0.84)
  waiting for transfers between devices: 112 us -> 85.5 us
  other arithmetic: 67.3 us -> 56.5 us
  local copies, waits for them, and re-layouts: 6.12 us -> 1.22 us
  matrix products: 19 us -> 14.4 us
    psum x1, waiting for transfers between devices: 110 us -> 51.4 us  [shards(): lax.psum((jnp.dot(data_anom.T, scaled, precision=highest), jnp.dot(scaled...]
    psum x0 -> x1, waiting for transfers between devices: none -> 31.8 us  [shards(): lax.psum(lax.psum((jnp.dot(data_anom.T, scaled, precision=highest), jnp.d...]
    another operation x7, other arithmetic: 37.8 us -> 29.5 us  [chol_apply(): factor = jnp.linalg.cholesky(system)]
    another operation x2, matrix products: 3.27 us -> 0.42 us  [chol_apply(): factor = jnp.linalg.cholesky(system)]
    another operation x6, other arithmetic: 22.8 us -> 20 us  [chol_apply(): lax.linalg.triangular_solve(factor, middle, left_side=True, lower=True, t...]
  transfers between devices with their start and end apart: 2 -> 3, of which waited for: 2 -> 3; matrix products, arithmetic and copies ran while one was open for 1% -> 2% of each run, Pallas kernels for 0% -> 0%
where the time goes in v1:
time: 233 us; the launch traced here: 232 us
  waiting for transfers between devices  85.5 us (37%)
  other arithmetic  56.5 us (24%)
  blocking collectives  55.7 us (24%)
  between operations  15.6 us (7%)
  matrix products  14.4 us (6%)
  starting transfers between devices  3.42 us (1%)
    psum x1, waiting for transfers between devices, shards(): lax.psum((jnp.dot(data_anom.T, scaled, precision=highest), jnp.dot(scaled...  51.4 us
    psum x1, waiting for transfers between devices, shards(): lax.psum(lax.psum((jnp.dot(data_anom.T, scaled, precision=highest), jnp.d...  31.8 us
    another operation x7, other arithmetic, chol_apply(): factor = jnp.linalg.cholesky(system)  29.5 us
    unnamed x1, blocking collectives  22.8 us
    another operation x6, other arithmetic, chol_apply(): lax.linalg.triangular_solve(factor, middle, left_side=True, lower=True, t...  20 us
    all_gather x1, blocking collectives, shards(): lax.all_gather(data_anom, 'tile', axis=0, tiled=True)  17.3 us
    all_gather x1, blocking collectives, shards(): lax.all_gather(gain_rows, 'tile', axis=0, tiled=True)  15.6 us
  transfers between devices with their start and end apart: 3, of which 3 were waited for; matrix products, arithmetic and copies ran while one was open for 2% of the time, Pallas kernels for 0%

profile of v1, /device:TPU:4, one launch (start us, length us, event | category | flops | bytes accessed | tf_op | source)
XLA Modules:
  0.0 232.3 jit_solution(6956525697917233292)
XLA Ops:
  6.5 0.0 all-reduce.10.cloned.1.call-start
  6.5 0.9 reduce_sum.18
  7.5 0.7 broadcast_multiply_fusion.1
  8.1 2.0 fusion.22
  10.1 2.0 fusion.21
  12.2 0.0 all-reduce.10.cloned.1.call-update
  12.2 0.0 all-reduce.12.cloned.1.call-start
  12.2 0.9 subtract_multiply_fusion.1
  13.1 0.7 multiply_bitcast_fusion
  13.8 0.1 broadcast_bitcast_fusion
  13.9 1.8 reduce_sum.19
  15.8 51.4 %all-reduce.10.cloned.1.call-done = (f32[200,200]{1,0:T(8,128)}, f32[200,200]{0,1:T(8,128)}) async-done(((f32[200,200]{1,0:T(8,128)}, f32[200,200]{0,1:T(8,128)}), (f32[200,200]{1,0:T(8,128)}, f32[200,200]{0,1:T(8,128)})) %all-reduce.10.cloned.1.call-update) | async-done | bytes 320016 | tf_op jit(solution)/shard_map/psum | solution.py:31
  67.2 0.0 all-reduce.12.cloned.1.call-update
  67.2 17.3 %all_gather.6 = f32[1024,200]{0,1:T(8,128)S(1)} all-gather(f32[128,200]{0,1:T(8,128)S(1)} %subtract_multiply_fusion.1), channel_id=1, replica_groups=mesh['well'=4,'tile'=8] {'tile'}, dimensions={0}, use_global_device_ids=true | all-gather | bytes 921600 | tf_op jit(solution)/shard_map/all_gather | solution.py:44
  84.5 31.8 %all-reduce.12.cloned.1.call-done = (f32[200,200]{1,0:T(8,128)}, f32[200,200]{0,1:T(8,128)}) async-done(((f32[200,200]{1,0:T(8,128)}, f32[200,200]{0,1:T(8,128)}), (f32[200,200]{1,0:T(8,128)}, f32[200,200]{0,1:T(8,128)})) %all-reduce.12.cloned.1.call-update) | async-done | bytes 320016 | tf_op jit(solution)/shard_map/psum | solution.py:30
  116.3 1.0 convert_add_fusion
  117.3 0.1 copy.10
  117.4 1.0 fusion.18
  118.4 11.7 %cholesky.51 = f32[128,128]{1,0:T(8,128)S(1)} custom-call(f32[128,128]{1,0:T(8,128)S(1)} %cholesky.124), custom_call_target="Cholesky" | custom-call | tf_op jit(solution)/shard_map/jit(cholesky)/cholesky | solution.py:10
  130.2 9.8 %custom-call.16 = f32[1,128,128]{1,2,0:T(8,128)S(1)} custom-call(f32[1,128,128]{2,1,0:T(8,128)S(1)} %get-tuple-element.32), custom_call_target="InvertDiagBlocksLowerTriangular" | custom-call | tf_op jit(solution)/shard_map/jit(cholesky)/cholesky | solution.py:10
  140.0 0.2 constant_dynamic-update-slice_fusion.1
  140.2 0.2 convolution_subtract_fusion.3
  140.4 6.6 %cholesky.110 = f32[72,72]{1,0:T(8,128)S(1)} custom-call(f32[72,72]{1,0:T(8,128)S(1)} %convolution_subtract_fusion.3), custom_call_target="Cholesky" | custom-call | tf_op jit(solution)/shard_map/jit(cholesky)/cholesky | solution.py:10
  147.1 0.7 compare_reduce_fusion
  147.7 0.6 compare_reduce_fusion.1
  149.7 0.0 copy-start.2
  149.7 0.1 fusion.23
  149.8 19.9 %custom-call.17 = f32[2,128,128]{1,2,0:T(8,128)S(1)} custom-call(f32[2,128,128]{2,1,0:T(8,128)S(1)} %pad_maximum_fusion), custom_call_target="InvertDiagBlocksLowerTriangular" | custom-call | tf_op jit(solution)/shard_map/triangular_solve | solution.py:14
  169.7 0.0 copy-start.4
  169.7 0.0 copy-done.5
  169.7 0.4 fusion.19
  170.1 0.0 copy-done.2
  170.1 0.2 copy-done.4
  170.3 0.3 convolution_subtract_fusion.2
  170.7 0.0 copy-start
  170.7 1.2 fusion.36
  171.9 1.0 fusion.35
  172.8 1.1 convolution_subtract_fusion
  174.0 1.2 fusion.26
  175.2 0.6 convolution_subtract_fusion.1
  175.8 15.6 %all_gather.7 = f32[1024,200]{0,1:T(8,128)S(1)} all-gather(f32[128,200]{0,1:T(8,128)S(1)} %convolution_subtract_fusion.1), channel_id=1, replica_groups=mesh['well'=4,'tile'=8] {'tile'}, dimensions={0}, use_global_device_ids=true | all-gather | bytes 921600 | tf_op jit(solution)/shard_map/all_gather | solution.py:45
  191.4 1.5 fusion.12
  192.9 22.8 %fusion = f32[200,64]{0,1:T(8,128)S(1)} fusion(f32[200,200]{0,1:T(8,128)} %fusion.12), kind=kCustom, calls=%all-reduce-scatter | all-reduce-scatter fusion | flops 51201 | bytes 211712
  215.8 3.4 %collective-permute-start = (f32[200,42]{0,1:T(8,128)S(1)}, f32[200,42]{0,1:T(8,128)S(1)}, u32[]{:S(2)}, u32[]{:S(2)}) collective-permute-start(f32[200,42]{0,1:T(8,128)S(1)} %slice.74), channel_id=1, source_target_pairs={{0,8},{8,16},{16,24},{1,9},{9,17},{17,25},{2,10},{10,18},{18,26},{... | collective-permute-start | bytes 100808
  219.2 0.6 dynamic-slice.8
  220.4 2.2 collective-permute-done
  222.7 0.2 concatenate.13
  222.9 2.6 %fusion.7 = f32[3,50,1024]{2,1,0:T(8,128)} fusion(f32[3,200,1024]{2,1,0:T(8,128)S(1)} %copy-done, f32[3,1024]{1,0:T(4,128)S(1)} %broadcast_multiply_fusion, s32[]{:T(128)S(6)} %select_n.7, f32[200,106]{0,1:T(8,128)S(1)} %concatenate.13, u32[]{:S(6)} %subtract.7), kind=kOutput, calls=%fused_computation.4 | convolution fusion | flops 370022400 | bytes 3833864 | tf_op jit(solution)/shard_map/vnc,nm->vmc/dot_general | solution.py:54
  (20 shorter events, 0.2 us)
Async XLA Ops:
  6.5 60.6 %all-reduce.10.cloned.1.call-start = ((), (), s32[]{:S(2)}) async-start(), calls=%async_computation | async-start | bytes 819200 | tf_op jit(solution)/shard_map/psum | solution.py:31
  12.2 104.1 %all-reduce.12.cloned.1.call-start = ((), (), s32[]{:S(2)}) async-start(), calls=%async_computation.1 | async-start | bytes 819200 | tf_op jit(solution)/shard_map/psum | solution.py:30
  116.3 53.4 %copy-start.5 = (f32[200,200]{1,0:T(8,128)S(1)}, f32[200,200]{1,0:T(8,128)}, u32[]{:S(2)}) copy-start(f32[200,200]{1,0:T(8,128)} %get-tuple-element.27) | copy-start | bytes 480004
  116.3 58.9 %copy-start.1 = (f32[128,200]{0,1:T(8,128)S(1)}, f32[128,200]{0,1:T(8,128)}, u32[]{:S(2)}) copy-start(f32[128,200]{0,1:T(8,128)} %param.7) | copy-start | bytes 307204
  116.3 58.9 %copy-start.3 = (f32[128,200]{0,1:T(8,128)S(1)}, f32[128,200]{0,1:T(8,128)}, u32[]{:S(2)}) copy-start(f32[128,200]{0,1:T(8,128)} %param.8) | copy-start | bytes 307204
  149.7 20.5 %copy-start.2 = (f32[200,200]{1,0:T(8,128)}, f32[200,200]{1,0:T(8,128)S(1)}, u32[]{:S(2)}) copy-start(f32[200,200]{1,0:T(8,128)S(1)} %select_select_fusion) | copy-start | bytes 480004
  169.7 0.7 copy-start.4
  170.3 48.8 %copy-start.6 = (u32[32]{0:T(128)S(1)}, u32[32]{0:T(128)}, u32[]{:S(2)}) copy-start(u32[32]{0:T(128)} %constant.155) | copy-start | bytes 388
  170.7 52.2 %copy-start = (f32[3,200,1024]{2,1,0:T(8,128)S(1)}, f32[3,200,1024]{2,1,0:T(8,128)}, u32[]{:S(2)}) copy-start(f32[3,200,1024]{2,1,0:T(8,128)} %param.6) | copy-start | bytes 7372804
  215.8 6.9 %collective-permute-start = (f32[200,42]{0,1:T(8,128)S(1)}, f32[200,42]{0,1:T(8,128)S(1)}, u32[]{:S(2)}, u32[]{:S(2)}) collective-permute-start(f32[200,42]{0,1:T(8,128)S(1)} %slice.74), channel_id=1, source_target_pairs={{0,8},{8,16},{16,24},{1,9},{9,17},{17,25},{2,10},{10,18},{18,26},{... | collective-permute-start | bytes 100808
Sparse Core Ops, SparseCore 0:
  12.3 54.8 all-reduce.9
  70.5 45.7 all-reduce.11
